TPU v7x, 32 devices: a whole 2x2x4 slice. The times are simulated.
32 devices in a mesh: groups: 2 (over y), frames: 4 (over z), heads: 4 (over x, core).
Axes of the slice: x: 2, y: 2, z: 4, core: 2. Of those that a mesh axis runs over, the one named last changes fastest.
Arguments:
- query_heads: bfloat16 [16384, 896], P(('groups', 'frames'), 'heads'), parts along dimension 0, may hold values from -6 to 6
- key_heads: bfloat16 [16384, 896], P(('groups', 'frames'), 'heads'), parts along dimension 0, may hold values from -0.04 to 8
- value_heads: bfloat16 [16384, 896], P(('groups', 'frames'), 'heads'), parts along dimension 0, may hold values from -6 to 6
- residual: bfloat16 [16384, 2240], P(('groups', 'frames', 'heads')), parts along dimension 0, may hold values from -6 to 6
- out_proj: bfloat16 [896, 2240], P('frames'), may hold values from -0.1875 to 0.1875
- frame_gate: float32 [32, 2240], P(('groups', 'frames')), parts along dimension 0, may hold values from -4 to 4
Outputs:
- updated: bfloat16 [16384, 2240], P(('groups', 'frames', 'heads')), parts along dimension 0
There are 2 independent parts, one for each index of `groups`. A program takes and returns all parts, laid end to end along the dimension named above; an argument that names none is the same for every part. Nothing has to cross between parts.
All inputs are finite; a program needn't handle non-finite values.
Results may differ from a plain program's by a relative error of at most 0.0033.
Values may be sent and summed in bfloat16 or wider, within the bound.
No kernel may reach another device: no remote copies, remote signals or barrier semaphores. Data moves between devices by JAX's collectives and lax.ppermute only.
A program may use at most 64 MiB of HBM per device.

v0:
```python
import jax
import jax.numpy as jnp
from jax import lax
from jax.sharding import PartitionSpec as P

HD = 112
HEADS_DEV = 2
FRAME_TOK = 512
EPSILON = 1e-06


def per_device(query_heads, key_heads, value_heads, residual, out_proj, frame_gate):
    length = query_heads.shape[0]
    frames_here = length // FRAME_TOK
    block_shape = (frames_here, FRAME_TOK, HEADS_DEV, HD)
    query_pos = jnp.maximum(query_heads, 0).reshape(block_shape)
    key_pos = jnp.maximum(key_heads, 0).reshape(block_shape)
    value_frames = value_heads.reshape(block_shape)
    frame_state = jnp.einsum(
        "fthi,fthj->fhij", key_pos, value_frames, preferred_element_type=jnp.float32
    )
    frame_sum = jnp.sum(key_pos, axis=1, dtype=jnp.float32)
    own_state = jnp.sum(frame_state, axis=0)
    own_sum = jnp.sum(frame_sum, axis=0)
    position = lax.axis_index("frames")
    gathered = (
        lax.all_gather(own_state[None], "frames", axis=0, tiled=True),
        lax.all_gather(own_sum[None], "frames", axis=0, tiled=True),
    )
    pieces = gathered[0].shape[0]
    is_lower = jnp.arange(pieces, dtype=jnp.int32) < position
    state_part = jnp.sum(jnp.where(is_lower[:, None, None, None], gathered[0], 0.0), axis=0)
    sum_part = jnp.sum(jnp.where(is_lower[:, None, None], gathered[1], 0.0), axis=0)
    prefix_state = state_part[None] + jnp.cumsum(frame_state, axis=0)
    prefix_sum = sum_part[None] + jnp.cumsum(frame_sum, axis=0)
    state_round = prefix_state.astype(jnp.bfloat16)
    sum_round = prefix_sum.astype(jnp.bfloat16)
    numerator = jnp.einsum(
        "fthi,fhij->fthj", query_pos, state_round, preferred_element_type=jnp.float32
    )
    denominator = (
        jnp.einsum("fthi,fhi->fth", query_pos, sum_round, preferred_element_type=jnp.float32)
        + EPSILON
    )
    attended = (
        (numerator / denominator[..., None]).astype(jnp.bfloat16).reshape(length, HEADS_DEV * HD)
    )
    rows_here = residual.shape[0]
    head_pos = lax.axis_index("heads")
    row_frame = (head_pos * rows_here + jnp.arange(rows_here, dtype=jnp.int32)) // FRAME_TOK
    selector = (row_frame[:, None] == jnp.arange(frames_here, dtype=jnp.int32)[None, :]).astype(
        jnp.float32
    )
    gate_rows = jnp.dot(
        selector, frame_gate, precision=lax.Precision.HIGHEST, preferred_element_type=jnp.float32
    )
    token_rows = lax.all_to_all(attended, "heads", split_axis=0, concat_axis=1, tiled=True)
    projected = jnp.dot(
        token_rows,
        lax.all_gather(out_proj, "frames", axis=0, tiled=True),
        preferred_element_type=jnp.float32,
    )
    return (residual.astype(jnp.float32) + gate_rows * projected).astype(jnp.bfloat16)


def solution(mesh):
    in_specs = (
        P(("groups", "frames"), "heads"),
        P(("groups", "frames"), "heads"),
        P(("groups", "frames"), "heads"),
        P(("groups", "frames", "heads"), None),
        P("frames", None),
        P(("groups", "frames"), None),
    )
    out_specs = P(("groups", "frames", "heads"), None)
    return jax.shard_map(
        per_device, mesh=mesh, in_specs=in_specs, out_specs=out_specs, check_vma=False
    )
```

profile of v0, /device:TPU:0, one launch (start us, length us, event | category | flops | bytes accessed | tf_op | source)
XLA Modules:
  0.0 113.2 jit_solution(14616134283706953128)
XLA Ops:
  6.5 0.7 all-gather.3.cloned.1.call-update
  7.3 1.4 %convert_reduce_fusion.1 = f32[224]{0:T(256)S(1)} fusion(bf16[2048,224]{0,1:T(8,128)(2,1)} %param.7), kind=kLoop, calls=%fused_computation.6 | loop fusion | flops 1376032 | bytes 918400 | tf_op jit(solution)/shard_map/reduce_sum | solution.py:24
  8.7 0.1 broadcast_in_dim.41
  8.8 1.2 %broadcast_maximum_fusion = bf16[2048,224]{0,1:T(8,128)(2,1)S(1)} fusion(bf16[2048,224]{0,1:T(8,128)(2,1)} %param.6), kind=kLoop, calls=%fused_computation.16 | loop fusion | flops 458752 | bytes 1835008 | tf_op jit(solution)/shard_map/max | solution.py:16
  10.0 0.7 reshape.48
  10.7 3.2 %reshape.47 = bf16[4,512,2,112]{1,0,3,2:T(4,128)(2,1)} reshape(bf16[2048,224]{0,1:T(8,128)(2,1)} %param.8) | data formatting | bytes 1835008 | tf_op jit(solution)/shard_map/reshape | solution.py:18
  13.9 0.1 broadcast_maximum_fusion.1
  14.0 0.7 reshape.46
  14.7 0.4 convert_reduce_fusion
  15.1 0.4 reduce_window_sum.23
  15.5 13.3 %all_gather.10 = f32[4,2,112]{2,1,0:T(2,128)S(1)} all-gather(f32[1,2,112]{2,1,0:T(2,128)S(1)} %broadcast_in_dim.41), channel_id=1, replica_groups=mesh['groups'=2,'frames'=4,'heads'=4] {'frames'}, dimensions={0}, use_global_device_ids=true | all-gather | bytes 4480 | tf_op jit(solution)/shard_map/all_gather | solution.py:28
  28.8 0.1 select_reduce_fusion.1
  28.9 0.1 fusion.12
  29.0 0.1 copy.16
  29.1 1.8 %fusion.17 = (f32[2,112,112]{2,1,0:T(8,128)S(1)}, f32[4,2,112,112]{3,2,1,0:T(8,128)S(1)}) fusion(bf16[4,512,2,112]{1,0,3,2:T(4,128)(2,1)} %reshape.47, bf16[4,512,2,112]{1,0,3,2:T(4,128)(2,1)S(1)} %reshape.46), kind=kOutput, calls=%fused_computation.36 | convolution fusion | flops 102835712 | bytes 2336768 | tf_op jit(solution)/shard_map/fthi,fthj->fhij/dot_general | solution.py:19
  30.9 19.9 %all-gather = f32[8,112,112]{2,1,0:T(8,128)S(1)} all-gather(f32[2,112,112]{2,1,0:T(8,128)S(1)} %get-tuple-element.5), channel_id=2, replica_groups=mesh['groups'=2,'frames'=4,'heads'=4] {'frames'}, dimensions={0}, use_global_device_ids=true | all-gather | bytes 501760 | tf_op jit(solution)/shard_map/all_gather | solution.py:27
  50.8 0.1 select_reduce_fusion
  50.9 0.4 fusion.7
  51.3 1.4 %fusion.2 = bf16[4,512,2,112]{1,3,2,0:T(8,128)(2,1)} fusion(bf16[4,2,112,112]{3,2,1,0:T(8,128)(2,1)S(1)} %fusion.3, f32[4,512,2]{1,2,0:T(2,128)S(1)} %fusion.13, bf16[4,512,2,112]{1,0,3,2:T(4,128)(2,1)S(1)} %reshape.48), kind=kOutput, calls=%fused_computation.4 | convolution fusion | flops 103677952 | bytes 2052096 | tf_op jit(solution)/shard_map/fthi,fhij->fthj/dot_general | solution.py:38
  52.7 3.6 %all-to-all-start = ((bf16[4,512,224]{1,2,0:T(8,128)(2,1)}), bf16[4,512,224]{1,2,0:T(8,128)(2,1)S(1)}, u32[]{:S(2)}, u32[]{:S(2)}) async-start(bf16[4,512,224]{1,2,0:T(8,128)(2,1)} %bitcast.5), calls=%async_computation | async-start | bytes 1835008 | tf_op jit(solution)/shard_map/all_to_all | solution.py:57
  56.4 4.1 %fusion.10 = f32[512,2240]{0,1:T(8,128)} fusion(f32[4,2240]{1,0:T(4,128)S(1)} %copy-done, s32[512]{0:T(512)S(1)} %add_select_fusion), kind=kOutput, calls=%fused_computation.19 | convolution fusion | flops 55052288 | bytes 4625408 | tf_op jit(solution)/shard_map/dot_general | solution.py:54
  60.5 8.8 %all-to-all-done = bf16[4,512,224]{1,2,0:T(8,128)(2,1)S(1)} async-done(((bf16[4,512,224]{1,2,0:T(8,128)(2,1)}), bf16[4,512,224]{1,2,0:T(8,128)(2,1)S(1)}, u32[]{:S(2)}, u32[]{:S(2)}) %all-to-all-start) | async-done | bytes 917536 | tf_op jit(solution)/shard_map/all_to_all | solution.py:57
  69.4 29.2 %all-gather.3.cloned.1.call-done = bf16[896,2240]{1,0:T(8,128)(2,1)} async-done(((bf16[224,2240]{1,0:T(8,128)(2,1)}), bf16[896,2240]{1,0:T(8,128)(2,1)}) %all-gather.3.cloned.1.call-update) | async-done | bytes 4014096 | tf_op jit(solution)/shard_map/all_gather | solution.py:60
  98.6 7.8 %fusion.1 = bf16[512,2240]{0,1:T(8,128)(2,1)} fusion(f32[512,2240]{0,1:T(8,128)} %fusion.10, bf16[512,896]{0,1:T(8,128)(2,1)S(1)} %bitcast.30, bf16[896,2240]{1,0:T(8,128)(2,1)} %all-gather.3.cloned.1.call-done, bf16[512,2240]{0,1:T(8,128)(2,1)S(1)} %copy-done.2), kind=kOutput, calls=%fused_computation.2 | convolution fusion | flops 2059796480 | bytes 14106624 | tf_op jit(solution)/shard_map/dot_general | solution.py:58
  (11 shorter events, 0.1 us)
Async XLA Ops:
  6.5 49.9 %copy-start = (f32[4,2240]{1,0:T(4,128)S(1)}, f32[4,2240]{1,0:T(4,128)}, u32[]{:S(2)}) copy-start(f32[4,2240]{1,0:T(4,128)} %param.11) | copy-start | bytes 107524
  6.5 7.4 %copy-start.1 = (bf16[2048,224]{0,1:T(8,128)(2,1)S(1)}, bf16[2048,224]{0,1:T(8,128)(2,1)}, u32[]{:S(2)}) copy-start(bf16[2048,224]{0,1:T(8,128)(2,1)} %param.7) | copy-start | bytes 2752516
  6.5 92.0 %all-gather.3.cloned.1.call-start = ((), (), s32[]{:S(2)}) async-start(), calls=%async_computation.1 | async-start | bytes 5160960 | tf_op jit(solution)/shard_map/all_gather | solution.py:60
  52.7 45.9 %copy-start.2 = (bf16[512,2240]{0,1:T(8,128)(2,1)S(1)}, bf16[512,2240]{0,1:T(8,128)(2,1)}, u32[]{:S(2)}) copy-start(bf16[512,2240]{0,1:T(8,128)(2,1)} %param.9) | copy-start | bytes 6881284
  52.7 16.6 %all-to-all-start = ((bf16[4,512,224]{1,2,0:T(8,128)(2,1)}), bf16[4,512,224]{1,2,0:T(8,128)(2,1)S(1)}, u32[]{:S(2)}, u32[]{:S(2)}) async-start(bf16[4,512,224]{1,2,0:T(8,128)(2,1)} %bitcast.5), calls=%async_computation | async-start | bytes 1835008 | tf_op jit(solution)/shard_map/all_to_all | solution.py:57
Sparse Core Ops, SparseCore 0:
  8.9 89.6 all-gather.2
where the time goes:
time: 114 us; the launch traced here: 113 us
  waiting for transfers between devices  38.8 us (34%)
  blocking collectives  33.1 us (29%)
  matrix products  15.5 us (14%)
  between operations  13.5 us (12%)
  local copies, waits for them, and re-layouts  4.76 us (4%)
  other arithmetic  3.95 us (3%)
  starting transfers between devices  3.64 us (3%)
    all_gather x1, waiting for transfers between devices, per_device(): lax.all_gather(out_proj, 'frames', axis=0, tiled=True)  29.2 us
    all_gather x1, blocking collectives, per_device(): lax.all_gather(own_state[None], 'frames', axis=0, tiled=True)  19.9 us
    all_gather x1, blocking collectives, per_device(): lax.all_gather(own_sum[None], 'frames', axis=0, tiled=True)  13.3 us
    all_to_all x1, waiting for transfers between devices, per_device(): lax.all_to_all(attended, 'heads', split_axis=0, concat_axis=1, tiled=True)  8.84 us
    dot_general x1, matrix products, per_device(): jnp.dot(token_rows, lax.all_gather(out_proj, 'frames', axis=0, tiled=True...  7.75 us
    dot_general x1, matrix products, per_device(): jnp.dot(selector, frame_gate, precision=lax.Precision.HIGHEST, preferred_...  4.13 us
    all_to_all x1, starting transfers between devices, per_device(): lax.all_to_all(attended, 'heads', split_axis=0, concat_axis=1, tiled=True)  3.64 us
    reshape x1, local copies, waits for them, and re-layouts, per_device(): value_frames = value_heads.reshape(block_shape)  3.23 us
  transfers between devices with their start and end apart: 2, of which 2 were waited for; matrix products, arithmetic and copies ran while one was open for 14% of the time, Pallas kernels for 0%

commit v1 on v0

--- a/solution.py
+++ b/solution.py
@@ -7,6 +7,24 @@
 HEADS_DEV = 2
 FRAME_TOK = 512
 EPSILON = 1e-06
+
+
+def collect(shard, axis, dim):
+    ways, here, hop = (lax.axis_size(axis), lax.axis_index(axis), shard.shape[dim])
+    shape = [n * ways if d == dim else n for d, n in enumerate(shard.shape)]
+    full = lax.dynamic_update_slice_in_dim(
+        jnp.zeros(shape, shard.dtype), shard, here * hop, axis=dim
+    )
+    going_up = going_down = shard
+    for far in range(1, ways // 2 + 1):
+        going_up = lax.ppermute(going_up, axis, [(d, (d + 1) % ways) for d in range(ways)])
+        full = lax.dynamic_update_slice_in_dim(full, going_up, (here - far) % ways * hop, axis=dim)
+        if 2 * far < ways:
+            going_down = lax.ppermute(going_down, axis, [(d, (d - 1) % ways) for d in range(ways)])
+            full = lax.dynamic_update_slice_in_dim(
+                full, going_down, (here + far) % ways * hop, axis=dim
+            )
+    return full
 
 
 def per_device(query_heads, key_heads, value_heads, residual, out_proj, frame_gate):
@@ -24,7 +42,7 @@
     own_sum = jnp.sum(frame_sum, axis=0)
     position = lax.axis_index("frames")
     gathered = (
-        lax.all_gather(own_state[None], "frames", axis=0, tiled=True),
+        collect(own_state[None], "frames", 0),
         lax.all_gather(own_sum[None], "frames", axis=0, tiled=True),
     )
     pieces = gathered[0].shape[0]

time: 114 us -> 110 us (0.965)
  blocking collectives: 33.1 us -> 9.95 us
  waiting for transfers between devices: 38.8 us -> 52.5 us
  starting transfers between devices: 3.64 us -> 8.9 us
    all_gather x1 -> x0, blocking collectives: 19.9 us -> none  [per_device(): lax.all_gather(own_state[None], 'frames', axis=0, tiled=True)]
    ppermute x0 -> x3, waiting for transfers between devices: none -> 8.29 us  [the longest x2 8.28 us: collect(): lax.ppermute(going_up, axis, [(d, (d + 1) % ways) for d in range(ways)])]
    all_gather x1, waiting for transfers between devices: 29.2 us -> 34.7 us  [per_device(): lax.all_gather(out_proj, 'frames', axis=0, tiled=True)]
    ppermute x0 -> x3, starting transfers between devices: none -> 5.25 us  [the longest x2 3.16 us: collect(): lax.ppermute(going_up, axis, [(d, (d + 1) % ways) for d in range(ways)])]
    all_gather x1, blocking collectives: 13.3 us -> 9.95 us  [per_device(): lax.all_gather(own_sum[None], 'frames', axis=0, tiled=True)]
    max x1, other arithmetic: 1.24 us -> 0.06 us  [per_device(): query_pos = jnp.maximum(query_heads, 0).reshape(block_shape)]
    reduce_sum x1, other arithmetic: 1.44 us -> 0.26 us  [per_device(): own_sum = jnp.sum(frame_sum, axis=0)]
    max x1, other arithmetic: 0.06 us -> 1.24 us  [per_device(): key_pos = jnp.maximum(key_heads, 0).reshape(block_shape)]
  transfers between devices with their start and end apart: 2 -> 5, of which waited for: 2 -> 3; matrix products, arithmetic and copies ran while one was open for 14% -> 15% of each run, Pallas kernels for 0% -> 0%
where the time goes in v1:
time: 110 us; the launch traced here: 109 us
  waiting for transfers between devices  52.5 us (48%)
  matrix products  15.6 us (14%)
  between operations  13.6 us (12%)
  blocking collectives  9.95 us (9%)
  starting transfers between devices  8.9 us (8%)
  local copies, waits for them, and re-layouts  5.84 us (5%)
  other arithmetic  3.02 us (3%)
    all_gather x1, waiting for transfers between devices, per_device(): lax.all_gather(out_proj, 'frames', axis=0, tiled=True)  34.7 us
    all_gather x1, blocking collectives, per_device(): lax.all_gather(own_sum[None], 'frames', axis=0, tiled=True)  9.95 us
    all_to_all x1, waiting for transfers between devices, per_device(): lax.all_to_all(attended, 'heads', split_axis=0, concat_axis=1, tiled=True)  8.83 us
    ppermute x2, waiting for transfers between devices, collect(): lax.ppermute(going_up, axis, [(d, (d + 1) % ways) for d in range(ways)])  8.28 us
    dot_general x1, matrix products, per_device(): jnp.dot(token_rows, lax.all_gather(out_proj, 'frames', axis=0, tiled=True...  7.75 us
    dot_general x1, matrix products, per_device(): jnp.dot(selector, frame_gate, precision=lax.Precision.HIGHEST, preferred_...  4.13 us
    all_to_all x1, starting transfers between devices, per_device(): lax.all_to_all(attended, 'heads', split_axis=0, concat_axis=1, tiled=True)  3.64 us
    reshape x1, local copies, waits for them, and re-layouts, per_device(): value_frames = value_heads.reshape(block_shape)  3.3 us
  transfers between devices with their start and end apart: 5, of which 3 were waited for; matrix products, arithmetic and copies ran while one was open for 15% of the time, Pallas kernels for 0%

profile of v1, /device:TPU:0, one launch (start us, length us, event | category | flops | bytes accessed | tf_op | source)
XLA Modules:
  0.0 109.4 jit_solution(10255176279395094350)
XLA Ops:
  6.5 0.7 all-gather.2.cloned.1.call-update
  7.3 3.3 %reshape.47 = bf16[4,512,2,112]{1,0,3,2:T(4,128)(2,1)} reshape(bf16[2048,224]{0,1:T(8,128)(2,1)} %param.8) | data formatting | bytes 1835008 | tf_op jit(solution)/shard_map/reshape | solution.py:36
  10.6 1.2 %broadcast_maximum_fusion.1 = bf16[2048,224]{0,1:T(8,128)(2,1)S(1)} fusion(bf16[2048,224]{0,1:T(8,128)(2,1)} %param.7), kind=kLoop, calls=%fused_computation.16 | loop fusion | flops 458752 | bytes 1835008 | tf_op jit(solution)/shard_map/max | solution.py:35
  11.8 0.7 reshape.46
  12.5 1.9 %fusion.17 = (f32[2,112,112]{2,1,0:T(8,128)S(1)}, f32[4,2,112,112]{3,2,1,0:T(8,128)S(1)}) fusion(bf16[4,512,2,112]{1,0,3,2:T(4,128)(2,1)} %reshape.47, bf16[4,512,2,112]{1,0,3,2:T(4,128)(2,1)S(1)} %reshape.46), kind=kOutput, calls=%fused_computation.40 | convolution fusion | flops 102835712 | bytes 2336768 | tf_op jit(solution)/shard_map/fthi,fthj->fhij/dot_general | solution.py:37
  14.4 3.1 %collective-permute-start = (f32[1,2,112,112]{3,2,1,0:T(8,128)S(1)}, f32[1,2,112,112]{3,2,1,0:T(8,128)S(1)}, u32[]{:S(2)}, u32[]{:S(2)}) collective-permute-start(f32[1,2,112,112]{3,2,1,0:T(8,128)S(1)} %bitcast.30), channel_id=1, source_target_pairs={{0,4},{4,8},{8,12},{12,0},{1,5},{5,9},{9,13},{13,1},{2,6},{6,10},{... | collective-permute-start | bytes 301064 | tf_op jit(solution)/shard_map/ppermute | solution.py:20
  17.5 2.1 %collective-permute-start.1 = (f32[1,2,112,112]{3,2,1,0:T(8,128)S(1)}, f32[1,2,112,112]{3,2,1,0:T(8,128)}, u32[]{:S(2)}, u32[]{:S(2)}) collective-permute-start(f32[1,2,112,112]{3,2,1,0:T(8,128)S(1)} %bitcast.31), channel_id=1, source_target_pairs={{0,12},{4,0},{8,4},{12,8},{1,13},{5,1},{9,5},{13,9},{2,14},{6,2},{... | collective-permute-start | bytes 301064 | tf_op jit(solution)/shard_map/ppermute | solution.py:23
  19.6 0.3 convert_reduce_fusion.1
  20.0 0.7 reshape.48
  20.7 0.4 convert_reduce_fusion
  21.1 0.4 reduce_window_sum.23
  21.5 10.0 %all_gather.6 = f32[4,2,112]{2,1,0:T(2,128)S(1)} all-gather(f32[1,2,112]{2,1,0:T(2,128)S(1)} %broadcast_in_dim.42), channel_id=1, replica_groups=mesh['groups'=2,'frames'=4,'heads'=4] {'frames'}, dimensions={0}, use_global_device_ids=true | all-gather | bytes 4480 | tf_op jit(solution)/shard_map/all_gather | solution.py:46
  31.7 0.1 copy.20
  31.8 0.3 fusion.18
  32.2 0.4 fusion.6
  32.7 0.9 constant_dynamic-update-slice_fusion.1
  33.6 8.3 %collective-permute-done.2 = f32[1,2,112,112]{3,2,1,0:T(8,128)S(1)} collective-permute-done((f32[1,2,112,112]{3,2,1,0:T(8,128)S(1)}, f32[1,2,112,112]{3,2,1,0:T(8,128)S(1)}, u32[]{:S(2)}, u32[]{:S(2)}) %collective-permute-start.2) | collective-permute-done | bytes 100384 | tf_op jit(solution)/shard_map/ppermute | solution.py:20
  41.9 0.1 select_reduce_fusion
  42.0 1.4 %fusion.2 = bf16[4,512,2,112]{1,3,2,0:T(8,128)(2,1)} fusion(f32[4,512,2]{1,2,0:T(2,128)S(1)} %fusion.13, bf16[4,512,2,112]{1,0,3,2:T(4,128)(2,1)S(1)} %reshape.48, f32[4,2,112,112]{3,2,1,0:T(8,128)S(1)} %fusion.18, f32[2,112,112]{2,1,0:T(8,128)S(1)} %select_reduce_fusion), kind=kOutput, calls=%fused_computation.4 | convolution fusion | flops 103878656 | bytes 2353152 | tf_op jit(solution)/shard_map/fthi,fhij->fthj/dot_general | solution.py:56
  43.5 3.6 %all-to-all-start = ((bf16[4,512,224]{1,2,0:T(8,128)(2,1)}), bf16[4,512,224]{1,2,0:T(8,128)(2,1)S(1)}, u32[]{:S(2)}, u32[]{:S(2)}) async-start(bf16[4,512,224]{1,2,0:T(8,128)(2,1)} %bitcast.5), calls=%async_computation | async-start | bytes 1835008 | tf_op jit(solution)/shard_map/all_to_all | solution.py:75
  47.1 4.1 %fusion.9 = f32[512,2240]{0,1:T(8,128)} fusion(f32[4,2240]{1,0:T(4,128)S(1)} %copy-done, s32[512]{0:T(512)S(1)} %add_select_fusion), kind=kOutput, calls=%fused_computation.18 | convolution fusion | flops 55052288 | bytes 4625408 | tf_op jit(solution)/shard_map/dot_general | solution.py:72
  51.3 8.8 %all-to-all-done = bf16[4,512,224]{1,2,0:T(8,128)(2,1)S(1)} async-done(((bf16[4,512,224]{1,2,0:T(8,128)(2,1)}), bf16[4,512,224]{1,2,0:T(8,128)(2,1)S(1)}, u32[]{:S(2)}, u32[]{:S(2)}) %all-to-all-start) | async-done | bytes 917536 | tf_op jit(solution)/shard_map/all_to_all | solution.py:75
  60.1 34.7 %all-gather.2.cloned.1.call-done = bf16[896,2240]{1,0:T(8,128)(2,1)} async-done(((bf16[224,2240]{1,0:T(8,128)(2,1)}), bf16[896,2240]{1,0:T(8,128)(2,1)}) %all-gather.2.cloned.1.call-update) | async-done | bytes 4014096 | tf_op jit(solution)/shard_map/all_gather | solution.py:78
  94.8 7.8 %fusion.1 = bf16[512,2240]{0,1:T(8,128)(2,1)} fusion(f32[512,2240]{0,1:T(8,128)} %fusion.9, bf16[512,896]{0,1:T(8,128)(2,1)S(1)} %bitcast.29, bf16[896,2240]{1,0:T(8,128)(2,1)} %all-gather.2.cloned.1.call-done, bf16[512,2240]{0,1:T(8,128)(2,1)S(1)} %copy-done.3), kind=kOutput, calls=%fused_computation.2 | convolution fusion | flops 2059796480 | bytes 14106624 | tf_op jit(solution)/shard_map/dot_general | solution.py:76
  (23 shorter events, 0.5 us)
Async XLA Ops:
  6.5 40.6 %copy-start = (f32[4,2240]{1,0:T(4,128)S(1)}, f32[4,2240]{1,0:T(4,128)}, u32[]{:S(2)}) copy-start(f32[4,2240]{1,0:T(4,128)} %param.11) | copy-start | bytes 107524
  6.5 88.2 %all-gather.2.cloned.1.call-start = ((), (), s32[]{:S(2)}) async-start(), calls=%async_computation.1 | async-start | bytes 5160960 | tf_op jit(solution)/shard_map/all_gather | solution.py:78
  7.3 12.3 %copy-start.1 = (bf16[2048,224]{0,1:T(8,128)(2,1)S(1)}, bf16[2048,224]{0,1:T(8,128)(2,1)}, u32[]{:S(2)}) copy-start(bf16[2048,224]{0,1:T(8,128)(2,1)} %param.7) | copy-start | bytes 2752516
  12.5 7.5 %copy-start.2 = (bf16[2048,224]{0,1:T(8,128)(2,1)S(1)}, bf16[2048,224]{0,1:T(8,128)(2,1)}, u32[]{:S(2)}) copy-start(bf16[2048,224]{0,1:T(8,128)(2,1)} %param.6) | copy-start | bytes 2752516
  14.4 18.2 %collective-permute-start = (f32[1,2,112,112]{3,2,1,0:T(8,128)S(1)}, f32[1,2,112,112]{3,2,1,0:T(8,128)S(1)}, u32[]{:S(2)}, u32[]{:S(2)}) collective-permute-start(f32[1,2,112,112]{3,2,1,0:T(8,128)S(1)} %bitcast.30), channel_id=1, source_target_pairs={{0,4},{4,8},{8,12},{12,0},{1,5},{5,9},{9,13},{13,1},{2,6},{6,10},{... | collective-permute-start | bytes 301064 | tf_op jit(solution)/shard_map/ppermute | solution.py:20
  17.5 15.2 %collective-permute-start.1 = (f32[1,2,112,112]{3,2,1,0:T(8,128)S(1)}, f32[1,2,112,112]{3,2,1,0:T(8,128)}, u32[]{:S(2)}, u32[]{:S(2)}) collective-permute-start(f32[1,2,112,112]{3,2,1,0:T(8,128)S(1)} %bitcast.31), channel_id=1, source_target_pairs={{0,12},{4,0},{8,4},{12,8},{1,13},{5,1},{9,5},{13,9},{2,14},{6,2},{... | collective-permute-start | bytes 301064 | tf_op jit(solution)/shard_map/ppermute | solution.py:23
  32.6 9.3 %collective-permute-start.2 = (f32[1,2,112,112]{3,2,1,0:T(8,128)S(1)}, f32[1,2,112,112]{3,2,1,0:T(8,128)S(1)}, u32[]{:S(2)}, u32[]{:S(2)}) collective-permute-start(f32[1,2,112,112]{3,2,1,0:T(8,128)S(1)} %collective-permute-done), channel_id=1, source_target_pairs={{0,4},{4,8},{8,12},{12,0},{1,5},{5,9},{9,13},{13,1},{2,6},{6,10},{... | collective-permute-start | bytes 301064 | tf_op jit(solution)/shard_map/ppermute | solution.py:20
  43.5 51.3 %copy-start.3 = (bf16[512,2240]{0,1:T(8,128)(2,1)S(1)}, bf16[512,2240]{0,1:T(8,128)(2,1)}, u32[]{:S(2)}) copy-start(bf16[512,2240]{0,1:T(8,128)(2,1)} %param.9) | copy-start | bytes 6881284
  43.5 16.6 %all-to-all-start = ((bf16[4,512,224]{1,2,0:T(8,128)(2,1)}), bf16[4,512,224]{1,2,0:T(8,128)(2,1)S(1)}, u32[]{:S(2)}, u32[]{:S(2)}) async-start(bf16[4,512,224]{1,2,0:T(8,128)(2,1)} %bitcast.5), calls=%async_computation | async-start | bytes 1835008 | tf_op jit(solution)/shard_map/all_to_all | solution.py:75
Sparse Core Ops, SparseCore 0:
  8.9 85.8 all-gather.1
